TPU v7x, 32 devices: a whole 2x2x4 slice. The times are simulated.
32 devices in a mesh: groups: 2 (over x), gz: 16 (over z, y, core).
Axes of the slice: x: 2, y: 2, z: 4, core: 2. Of those that a mesh axis runs over, the one named last changes fastest.
Arguments:
- waves: bfloat16 [192, 8, 64, 256], P(('groups', 'gz')), parts along dimension 0, may hold values from -6 to 6
- potential: float32 [192, 512], P(('groups', 'gz')), parts along dimension 0, may hold values from 0.25 to 4
- domain_of: int32 [32], P('groups'), parts along dimension 0, may hold values from 0 to 7, never falling along the last dimension, each value on 1 to 9 neighbouring positions
Outputs:
- orbitals: bfloat16 [192, 8, 64, 256], P(('groups', 'gz')), parts along dimension 0
There are 2 independent parts, one for each index of `groups`. A program takes and returns all parts, laid end to end along the dimension named above; each array names one. Nothing has to cross between parts.
Inputs may be any that keep to these rules, and one draw needn't show every extreme that they name: `domain_of`: never falls; every domain holds 1 to 9 blocks, one domain exactly that many.
All inputs are finite; a program needn't handle non-finite values.
Results may differ from a plain program's by a relative error of at most 0.0038.
The roundings to bfloat16 on the way count: a program that leaves them out, or rounds other values in their place, can miss the bound.
Values may be sent and summed in bfloat16 or wider, within the bound.
No kernel may reach another device: no remote copies, remote signals or barrier semaphores. Data moves between devices by JAX's collectives and lax.ppermute only.
A program may use at most 64 MiB of HBM per device.

v0:
```python
import jax
import jax.numpy as jnp
from jax import lax
from jax.sharding import PartitionSpec as P

PANEL = 128
NX = 64
NY = 8
DOMS = 8
DEGREE = 4
COEF = (-49.0 / 18.0, 1.5, -0.15, 1.0 / 90.0)
CSHIFT = 7.0
EWIDTH = 5.0


def extended_2(block, sides, width):
    for axis, dim in sides:
        count = lax.axis_size(axis)
        forward = [(i, i + 1) for i in range(count - 1)]
        backward = [(target, source) for source, target in forward]
        low = lax.ppermute(
            lax.slice_in_dim(block, block.shape[dim] - width, None, axis=dim), axis, forward
        )
        high = lax.ppermute(lax.slice_in_dim(block, 0, width, axis=dim), axis, backward)
        block = jnp.concatenate([low, block, high], axis=dim)
    return block


def hamiltonian(extended, potential):
    inner = extended[3:-3]
    planes = inner.shape[0]
    rows_y = inner.shape[1]
    rows_x = inner.shape[2]
    padded_y = jnp.pad(inner, ((0, 0), (3, 3), (0, 0), (0, 0)))
    padded_x = jnp.pad(inner, ((0, 0), (0, 0), (3, 3), (0, 0)))
    total = 3.0 * COEF[0] * inner
    for distance in (1, 2, 3):
        along_z = (
            extended[3 + distance : 3 + distance + planes]
            + extended[3 - distance : 3 - distance + planes]
        )
        along_y = (
            padded_y[:, 3 + distance : 3 + distance + rows_y]
            + padded_y[:, 3 - distance : 3 - distance + rows_y]
        )
        along_x = (
            padded_x[:, :, 3 + distance : 3 + distance + rows_x]
            + padded_x[:, :, 3 - distance : 3 - distance + rows_x]
        )
        total = total + COEF[distance] * (along_z + along_y + along_x)
    return potential[:, :, :, None] * inner - 0.5 * total


def shards(waves, potential, domain_of):
    slabs = lax.axis_size("gz")
    position = lax.axis_index("gz")
    planes = waves.shape[0]
    bands = waves.shape[3]
    grid = potential.reshape(planes, NY, NX)
    owner = domain_of[position]
    below = jnp.where(position > 0, domain_of[jnp.maximum(position - 1, 0)] == owner, False).astype(
        jnp.float32
    )
    above = jnp.where(
        position < slabs - 1, domain_of[jnp.minimum(position + 1, slabs - 1)] == owner, False
    ).astype(jnp.float32)
    mask_three = jnp.concatenate(
        [
            jnp.broadcast_to(below, (3,)),
            jnp.ones((planes,), jnp.float32),
            jnp.broadcast_to(above, (3,)),
        ]
    )[:, None, None, None]

    def rimmed(field):
        return extended_2(field, (("gz", 0),), 3).astype(jnp.float32) * mask_three

    extended = rimmed(waves)
    image = hamiltonian(extended, grid)
    older = waves
    current = ((image - CSHIFT * extended[3:-3]) / EWIDTH).astype(jnp.bfloat16)
    for turn in range(DEGREE - 1):
        extended = rimmed(current)
        image = hamiltonian(extended, grid)
        newer = (
            2.0 / EWIDTH * (image - CSHIFT * extended[3:-3]) - older.astype(jnp.float32)
        ).astype(jnp.bfloat16)
        older, current = (current, newer)
    cells = jnp.sum((domain_of == owner).astype(jnp.float32)) * (planes * NY * NX)
    rows = current.reshape(planes * NY * NX, bands)

    def domain_total(term):
        picker = (jnp.arange(DOMS) == owner).astype(jnp.float32)
        summed = lax.psum(picker[:, None, None] * term[None], "gz")
        return jnp.sum(picker[:, None, None] * summed, axis=0)

    identity = jnp.eye(PANEL, dtype=jnp.float32)
    pieces = []
    for panel in range(bands // PANEL):
        block = rows[:, panel * PANEL : (panel + 1) * PANEL]
        if panel > 0:
            earlier = pieces[0]
            correlation = (
                domain_total(
                    jnp.einsum("ca,cb->ab", earlier, block, preferred_element_type=jnp.float32)
                )
                / cells
            )
            block = (
                block.astype(jnp.float32)
                - jnp.dot(
                    earlier, correlation.astype(jnp.bfloat16), preferred_element_type=jnp.float32
                )
            ).astype(jnp.bfloat16)
        gram = (
            domain_total(jnp.einsum("ca,cb->ab", block, block, preferred_element_type=jnp.float32))
            / cells
        )
        factor = jnp.linalg.cholesky(gram)
        inverse = jax.scipy.linalg.solve_triangular(factor, identity, lower=True)
        whitening = inverse.T.astype(jnp.bfloat16)
        pieces.append(
            jnp.dot(block, whitening, preferred_element_type=jnp.float32).astype(jnp.bfloat16)
        )
    return jnp.concatenate(pieces, axis=1).reshape(planes, NY, NX, bands)


def solution(mesh):
    return jax.shard_map(
        shards,
        mesh=mesh,
        in_specs=(P(("groups", "gz"), None, None, None), P(("groups", "gz"), None), P("groups")),
        out_specs=P(("groups", "gz"), None, None, None),
        check_vma=False,
    )
```

profile of v0, /device:TPU:0, one launch (start us, length us, event | category | flops | bytes accessed | tf_op | source)
XLA Modules:
  0.0 492.9 jit_solution(13511593628192767567)
XLA Ops:
  6.5 2.8 fusion.114
  9.3 2.4 collective-permute-start
  11.8 1.3 collective-permute-start.1
  13.1 0.7 fusion.115
  16.2 2.0 collective-permute-done.1
  18.3 0.7 convert_multiply_fusion.3
  19.2 6.6 %fusion.11 = bf16[6,8,64,256]{3,2,1,0:T(8,128)(2,1)S(1)} fusion(f32[6,8,64,256]{3,2,1,0:T(8,128)S(1)} %slice.356, f32[12,8,64,256]{3,2,1,0:T(8,128)S(1)} %convert_multiply_fusion.3, f32[6,8,64]{2,1,0:T(8,128)S(1)} %mul.191), kind=kLoop, calls=%fused_computation.66 | loop fusion | flops 22806528 | bytes 23605248 | tf_op jit(solution)/shard_map/convert_element_type | solution.py:81
  26.0 15.7 %collective-permute-start.2 = (bf16[3,8,64,256]{3,2,1,0:T(8,128)(2,1)S(1)}, bf16[3,8,64,256]{3,2,1,0:T(8,128)(2,1)S(1)}, u32[]{:S(2)}, u32[]{:S(2)}) collective-permute-start(bf16[3,8,64,256]{3,2,1,0:T(8,128)(2,1)S(1)} %get-tuple-element.11), channel_id=1, source_target_pairs={{0,1},{1,2},{2,3},{3,4},{4,5},{5,6},{6,7},{7,8},{8,9},{9,10},{10,1... | collective-permute-start | bytes 2359304 | tf_op jit(solution)/shard_map/ppermute | solution.py:21
  41.7 1.3 collective-permute-start.3
  43.0 0.5 collective-permute-done.2
  43.5 4.2 collective-permute-done.3
  47.7 0.7 convert_multiply_fusion.2
  48.5 2.0 slice.365
  50.5 18.8 %fusion.95 = bf16[6,8,64,256]{3,2,1,0:T(8,128)(2,1)S(1)} fusion(bf16[6,8,64,256]{3,2,1,0:T(8,128)(2,1)S(1)} %copy-done, f32[6,8,64,256]{3,2,1,0:T(8,128)} %slice.365, f32[12,8,64,256]{3,2,1,0:T(8,128)S(1)} %convert_multiply_fusion.2, f32[6,8,64]{2,1,0:T(8,128)S(1)} %mul.191), kind=kLoop, calls=%fused_computation.162 | loop fusion | flops 24379392 | bytes 25178112 | tf_op jit(solution)/shard_map/convert_element_type | solution.py:87
  69.5 15.6 %collective-permute-start.4 = (bf16[3,8,64,256]{3,2,1,0:T(8,128)(2,1)S(1)}, bf16[3,8,64,256]{3,2,1,0:T(8,128)(2,1)S(1)}, u32[]{:S(2)}, u32[]{:S(2)}) collective-permute-start(bf16[3,8,64,256]{3,2,1,0:T(8,128)(2,1)S(1)} %get-tuple-element.9), channel_id=1, source_target_pairs={{0,1},{1,2},{2,3},{3,4},{4,5},{5,6},{6,7},{7,8},{8,9},{9,10},{10,1... | collective-permute-start | bytes 2359304 | tf_op jit(solution)/shard_map/ppermute | solution.py:21
  85.1 1.3 collective-permute-start.5
  86.4 0.5 collective-permute-done.4
  87.0 4.3 collective-permute-done.5
  91.2 0.7 convert_multiply_fusion.1
  92.0 2.0 slice.374
  94.0 18.8 %fusion.94 = bf16[6,8,64,256]{3,2,1,0:T(8,128)(2,1)S(1)} fusion(bf16[6,8,64,256]{3,2,1,0:T(8,128)(2,1)S(1)} %fusion.11, f32[6,8,64,256]{3,2,1,0:T(8,128)} %slice.374, f32[12,8,64,256]{3,2,1,0:T(8,128)S(1)} %convert_multiply_fusion.1, f32[6,8,64]{2,1,0:T(8,128)S(1)} %mul.191), kind=kLoop, calls=%fused_computation.161 | loop fusion | flops 24379392 | bytes 25178112 | tf_op jit(solution)/shard_map/convert_element_type | solution.py:87
  113.0 15.6 %collective-permute-start.6 = (bf16[3,8,64,256]{3,2,1,0:T(8,128)(2,1)S(1)}, bf16[3,8,64,256]{3,2,1,0:T(8,128)(2,1)S(1)}, u32[]{:S(2)}, u32[]{:S(2)}) collective-permute-start(bf16[3,8,64,256]{3,2,1,0:T(8,128)(2,1)S(1)} %get-tuple-element.6), channel_id=1, source_target_pairs={{0,1},{1,2},{2,3},{3,4},{4,5},{5,6},{6,7},{7,8},{8,9},{9,10},{10,1... | collective-permute-start | bytes 2359304 | tf_op jit(solution)/shard_map/ppermute | solution.py:21
  128.7 1.3 collective-permute-start.7
  130.0 0.5 compare_convert_fusion.1
  130.5 4.3 collective-permute-done.7
  134.8 0.7 convert_multiply_fusion
  135.9 6.8 %fusion.93 = bf16[6,8,64,256]{3,2,1,0:T(8,128)(2,1)S(1)} fusion(bf16[6,8,64,256]{3,2,1,0:T(8,128)(2,1)S(1)} %fusion.95, f32[6,8,64,256]{3,2,1,0:T(8,128)S(1)} %slice.383, f32[12,8,64,256]{3,2,1,0:T(8,128)S(1)} %convert_multiply_fusion, f32[6,8,64]{2,1,0:T(8,128)S(1)} %mul.191), kind=kLoop, calls=%fused_computation.160 | loop fusion | flops 24379392 | bytes 25178112 | tf_op jit(solution)/shard_map/convert_element_type | solution.py:87
  143.0 0.9 broadcast_multiply_fusion.2
  144.2 1.2 fusion.110
  146.1 101.4 %all-reduce.12.cloned.1.call-done = f32[8,128,128]{2,1,0:T(8,128)} async-done(((f32[8,128,128]{2,1,0:T(8,128)}), f32[8,128,128]{2,1,0:T(8,128)}) %all-reduce.12.cloned.1.call-update) | async-done | bytes 524304 | tf_op jit(solution)/shard_map/psum | solution.py:94
  247.5 1.1 multiply_reduce_fusion.2
  248.9 11.7 %cholesky.44 = f32[128,128]{1,0:T(8,128)S(1)} custom-call(f32[128,128]{1,0:T(8,128)S(1)} %fusion.108), custom_call_target="Cholesky" | custom-call | tf_op jit(solution)/shard_map/jit(cholesky)/cholesky | solution.py:119
  260.6 0.6 compare_reduce_fusion.1
  261.3 0.7 fusion.103
  262.0 9.8 %custom-call.6 = f32[1,128,128]{1,2,0:T(8,128)S(1)} custom-call(f32[1,128,128]{2,1,0:T(8,128)S(1)} %fusion.103), custom_call_target="InvertDiagBlocksLowerTriangular" | custom-call | tf_op jit(solution)/shard_map/jit(_solve_triangular)/triangular_solve | solution.py:120
  272.8 0.9 broadcast_multiply_fusion.1
  274.0 91.0 %all-reduce.14.cloned.1.call-done = f32[8,128,128]{2,1,0:T(8,128)} async-done(((f32[8,128,128]{2,1,0:T(8,128)}), f32[8,128,128]{2,1,0:T(8,128)}) %all-reduce.14.cloned.1.call-update) | async-done | bytes 524304 | tf_op jit(solution)/shard_map/psum | solution.py:94
  365.0 1.1 multiply_reduce_fusion.1
  366.3 0.4 fusion
  366.7 0.4 fusion.116
  367.1 0.9 broadcast_multiply_fusion
  368.0 91.8 %all-reduce.16.cloned.1.call-done = f32[8,128,128]{2,1,0:T(8,128)} async-done(((f32[8,128,128]{2,1,0:T(8,128)}), f32[8,128,128]{2,1,0:T(8,128)}) %all-reduce.16.cloned.1.call-update) | async-done | bytes 524304 | tf_op jit(solution)/shard_map/psum | solution.py:94
  459.8 1.1 multiply_reduce_fusion
  461.2 11.7 %cholesky.55 = f32[128,128]{1,0:T(8,128)S(1)} custom-call(f32[128,128]{1,0:T(8,128)S(1)} %fusion.106), custom_call_target="Cholesky" | custom-call | tf_op jit(solution)/shard_map/jit(cholesky)/cholesky | solution.py:119
  472.9 0.6 compare_reduce_fusion
  473.6 0.7 fusion.104
  474.2 9.8 %custom-call.7 = f32[1,128,128]{1,2,0:T(8,128)S(1)} custom-call(f32[1,128,128]{2,1,0:T(8,128)S(1)} %fusion.104), custom_call_target="InvertDiagBlocksLowerTriangular" | custom-call | tf_op jit(solution)/shard_map/jit(_solve_triangular)/triangular_solve | solution.py:120
  484.8 1.6 copy.15
  (42 shorter events, 4.5 us)
Async XLA Ops:
  6.5 11.7 %copy-start = (bf16[6,8,64,256]{3,2,1,0:T(8,128)(2,1)S(1)}, bf16[6,8,64,256]{3,2,1,0:T(8,128)(2,1)}, u32[]{:S(2)}) copy-start(bf16[6,8,64,256]{3,2,1,0:T(8,128)(2,1)} %param.6) | copy-start | bytes 4718596
  6.5 6.6 %copy-start.2 = (s32[16]{0:T(128)S(1)}, s32[16]{0:T(128)}, u32[]{:S(2)}) copy-start(s32[16]{0:T(128)} %param.8) | copy-start | bytes 196
  6.5 9.5 %copy-start.1 = (f32[6,512]{1,0:T(8,128)S(1)}, f32[6,512]{1,0:T(8,128)}, u32[]{:S(2)}) copy-start(f32[6,512]{1,0:T(8,128)} %param.7) | copy-start | bytes 36868
  6.5 241.0 %all-reduce.12.cloned.1.call-start = ((), (), s32[]{:S(2)}) async-start(), calls=%async_computation | async-start | bytes 1048576 | tf_op jit(solution)/shard_map/psum | solution.py:94
  9.3 6.9 %collective-permute-start = (bf16[3,8,64,256]{3,2,1,0:T(8,128)(2,1)}, bf16[3,8,64,256]{3,2,1,0:T(8,128)(2,1)S(1)}, u32[]{:S(2)}, u32[]{:S(2)}) collective-permute-start(bf16[3,8,64,256]{3,2,1,0:T(8,128)(2,1)} %get-tuple-element.13), channel_id=1, source_target_pairs={{0,1},{1,2},{2,3},{3,4},{4,5},{5,6},{6,7},{7,8},{8,9},{9,10},{10,1... | collective-permute-start | bytes 2359304 | tf_op jit(solution)/shard_map/ppermute | solution.py:21
  11.8 6.5 %collective-permute-start.1 = (bf16[3,8,64,256]{3,2,1,0:T(8,128)(2,1)}, bf16[3,8,64,256]{3,2,1,0:T(8,128)(2,1)S(1)}, u32[]{:S(2)}, u32[]{:S(2)}) collective-permute-start(bf16[3,8,64,256]{3,2,1,0:T(8,128)(2,1)} %get-tuple-element.14), channel_id=1, source_target_pairs={{1,0},{2,1},{3,2},{4,3},{5,4},{6,5},{7,6},{8,7},{9,8},{10,9},{11,1... | collective-permute-start | bytes 2359304 | tf_op jit(solution)/shard_map/ppermute | solution.py:24
  26.0 17.6 %collective-permute-start.2 = (bf16[3,8,64,256]{3,2,1,0:T(8,128)(2,1)S(1)}, bf16[3,8,64,256]{3,2,1,0:T(8,128)(2,1)S(1)}, u32[]{:S(2)}, u32[]{:S(2)}) collective-permute-start(bf16[3,8,64,256]{3,2,1,0:T(8,128)(2,1)S(1)} %get-tuple-element.11), channel_id=1, source_target_pairs={{0,1},{1,2},{2,3},{3,4},{4,5},{5,6},{6,7},{7,8},{8,9},{9,10},{10,1... | collective-permute-start | bytes 2359304 | tf_op jit(solution)/shard_map/ppermute | solution.py:21
  41.7 6.0 %collective-permute-start.3 = (bf16[3,8,64,256]{3,2,1,0:T(8,128)(2,1)S(1)}, bf16[3,8,64,256]{3,2,1,0:T(8,128)(2,1)S(1)}, u32[]{:S(2)}, u32[]{:S(2)}) collective-permute-start(bf16[3,8,64,256]{3,2,1,0:T(8,128)(2,1)S(1)} %get-tuple-element.12), channel_id=1, source_target_pairs={{1,0},{2,1},{3,2},{4,3},{5,4},{6,5},{7,6},{8,7},{9,8},{10,9},{11,1... | collective-permute-start | bytes 2359304 | tf_op jit(solution)/shard_map/ppermute | solution.py:24
  69.5 17.5 %collective-permute-start.4 = (bf16[3,8,64,256]{3,2,1,0:T(8,128)(2,1)S(1)}, bf16[3,8,64,256]{3,2,1,0:T(8,128)(2,1)S(1)}, u32[]{:S(2)}, u32[]{:S(2)}) collective-permute-start(bf16[3,8,64,256]{3,2,1,0:T(8,128)(2,1)S(1)} %get-tuple-element.9), channel_id=1, source_target_pairs={{0,1},{1,2},{2,3},{3,4},{4,5},{5,6},{6,7},{7,8},{8,9},{9,10},{10,1... | collective-permute-start | bytes 2359304 | tf_op jit(solution)/shard_map/ppermute | solution.py:21
  85.1 6.1 %collective-permute-start.5 = (bf16[3,8,64,256]{3,2,1,0:T(8,128)(2,1)S(1)}, bf16[3,8,64,256]{3,2,1,0:T(8,128)(2,1)S(1)}, u32[]{:S(2)}, u32[]{:S(2)}) collective-permute-start(bf16[3,8,64,256]{3,2,1,0:T(8,128)(2,1)S(1)} %get-tuple-element.10), channel_id=1, source_target_pairs={{1,0},{2,1},{3,2},{4,3},{5,4},{6,5},{7,6},{8,7},{9,8},{10,9},{11,1... | collective-permute-start | bytes 2359304 | tf_op jit(solution)/shard_map/ppermute | solution.py:24
  113.0 17.5 %collective-permute-start.6 = (bf16[3,8,64,256]{3,2,1,0:T(8,128)(2,1)S(1)}, bf16[3,8,64,256]{3,2,1,0:T(8,128)(2,1)S(1)}, u32[]{:S(2)}, u32[]{:S(2)}) collective-permute-start(bf16[3,8,64,256]{3,2,1,0:T(8,128)(2,1)S(1)} %get-tuple-element.6), channel_id=1, source_target_pairs={{0,1},{1,2},{2,3},{3,4},{4,5},{5,6},{6,7},{7,8},{8,9},{9,10},{10,1... | collective-permute-start | bytes 2359304 | tf_op jit(solution)/shard_map/ppermute | solution.py:21
  128.7 6.1 %collective-permute-start.7 = (bf16[3,8,64,256]{3,2,1,0:T(8,128)(2,1)S(1)}, bf16[3,8,64,256]{3,2,1,0:T(8,128)(2,1)S(1)}, u32[]{:S(2)}, u32[]{:S(2)}) collective-permute-start(bf16[3,8,64,256]{3,2,1,0:T(8,128)(2,1)S(1)} %get-tuple-element.8), channel_id=1, source_target_pairs={{1,0},{2,1},{3,2},{4,3},{5,4},{6,5},{7,6},{8,7},{9,8},{10,9},{11,1... | collective-permute-start | bytes 2359304 | tf_op jit(solution)/shard_map/ppermute | solution.py:24
  144.0 221.1 %all-reduce.14.cloned.1.call-start = ((), (), s32[]{:S(2)}) async-start(), calls=%async_computation.1 | async-start | bytes 1048576 | tf_op jit(solution)/shard_map/psum | solution.py:94
  273.7 186.1 %all-reduce.16.cloned.1.call-start = ((), (), s32[]{:S(2)}) async-start(), calls=%async_computation.2 | async-start | bytes 1048576 | tf_op jit(solution)/shard_map/psum | solution.py:94
Sparse Core Ops, SparseCore 0:
  144.1 103.3 all-reduce.11
  273.8 91.1 all-reduce.13
  368.4 91.3 all-reduce.15
where the time goes:
time: 493 us
  waiting for transfers between devices  300 us (61%)
  other arithmetic  108 us (22%)
  starting transfers between devices  55 us (11%)
  between operations  16.5 us (3%)
  local copies, waits for them, and re-layouts  10.7 us (2%)
    psum x3, waiting for transfers between devices, domain_total(): summed = lax.psum(picker[:, None, None] * term[None], 'gz')  284 us
    ppermute x4, starting transfers between devices, extended_2(): lax.ppermute(lax.slice_in_dim(block, block.shape[dim] - width, None, axis...  49.4 us
    convert_element_type x3, other arithmetic, shards(): newer = (2.0 / EWIDTH * (image - CSHIFT * extended[3:-3]) - older.astype(...  44.4 us
    another operation x6, other arithmetic, shards(): factor = jnp.linalg.cholesky(gram)  24.8 us
    another operation x4, other arithmetic, shards(): inverse = jax.scipy.linalg.solve_triangular(factor, identity, lower=True)  20.9 us
    ppermute x4, waiting for transfers between devices, extended_2(): lax.ppermute(lax.slice_in_dim(block, 0, width, axis=dim), axis, backward)  14.7 us
  transfers between devices with their start and end apart: 11, of which 9 were waited for; matrix products, arithmetic and copies ran while one was open for 1% of the time, Pallas kernels for 0%

commit v1 on v0

--- a/solution.py
+++ b/solution.py
@@ -1,3 +1,4 @@
+import functools
 import jax
 import jax.numpy as jnp
 from jax import lax
@@ -11,6 +12,14 @@
 COEF = (-49.0 / 18.0, 1.5, -0.15, 1.0 / 90.0)
 CSHIFT = 7.0
 EWIDTH = 5.0
+
+
+def row_guide(xin, which_axis):
+    res = lax.all_gather(xin, which_axis)
+    return jnp.sum(res, axis=0)
+
+
+balance_the_chains = functools.partial(row_guide, which_axis="gz")
 
 
 def extended_2(block, sides, width):
@@ -91,7 +100,7 @@
 
     def domain_total(term):
         picker = (jnp.arange(DOMS) == owner).astype(jnp.float32)
-        summed = lax.psum(picker[:, None, None] * term[None], "gz")
+        summed = balance_the_chains(picker[:, None, None] * term[None])
         return jnp.sum(picker[:, None, None] * summed, axis=0)
 
     identity = jnp.eye(PANEL, dtype=jnp.float32)

time: 493 us -> 449 us (0.911)
  waiting for transfers between devices: 300 us -> 247 us
  other arithmetic: 108 us -> 116 us
    psum x3 -> x0, waiting for transfers between devices: 284 us -> none  [domain_total(): summed = lax.psum(picker[:, None, None] * term[None], 'gz')]
    all_gather x0 -> x3, waiting for transfers between devices: none -> 231 us  [row_guide(): res = lax.all_gather(xin, which_axis)]
    reduce_sum x0 -> x3, other arithmetic: none -> 11.8 us  [row_guide(): return jnp.sum(res, axis=0)]
where the time goes in v1:
time: 449 us; the launch traced here: 448 us
  waiting for transfers between devices  247 us (55%)
  other arithmetic  116 us (26%)
  starting transfers between devices  55 us (12%)
  between operations  16.5 us (4%)
  local copies, waits for them, and re-layouts  10.7 us (2%)
    all_gather x3, waiting for transfers between devices, row_guide(): res = lax.all_gather(xin, which_axis)  231 us
    ppermute x4, starting transfers between devices, extended_2(): lax.ppermute(lax.slice_in_dim(block, block.shape[dim] - width, None, axis...  49.4 us
    convert_element_type x3, other arithmetic, shards(): newer = (2.0 / EWIDTH * (image - CSHIFT * extended[3:-3]) - older.astype(...  44.4 us
    another operation x6, other arithmetic, shards(): factor = jnp.linalg.cholesky(gram)  24.8 us
    another operation x4, other arithmetic, shards(): inverse = jax.scipy.linalg.solve_triangular(factor, identity, lower=True)  20.9 us
    ppermute x4, waiting for transfers between devices, extended_2(): lax.ppermute(lax.slice_in_dim(block, 0, width, axis=dim), axis, backward)  14.6 us
    reduce_sum x3, other arithmetic, row_guide(): return jnp.sum(res, axis=0)  11.8 us
  transfers between devices with their start and end apart: 11, of which 9 were waited for; matrix products, arithmetic and copies ran while one was open for 1% of the time, Pallas kernels for 0%

profile of v1, /device:TPU:0, one launch (start us, length us, event | category | flops | bytes accessed | tf_op | source)
XLA Modules:
  0.0 448.2 jit_solution(7298900746538987689)
XLA Ops:
  6.5 2.8 fusion.114
  9.3 2.4 collective-permute-start
  11.8 1.3 collective-permute-start.1
  13.1 0.7 fusion.115
  16.3 2.0 collective-permute-done.1
  18.3 0.7 convert_multiply_fusion.3
  19.2 6.6 %fusion.11 = bf16[6,8,64,256]{3,2,1,0:T(8,128)(2,1)S(1)} fusion(f32[6,8,64,256]{3,2,1,0:T(8,128)S(1)} %slice.356, f32[12,8,64,256]{3,2,1,0:T(8,128)S(1)} %convert_multiply_fusion.3, f32[6,8,64]{2,1,0:T(8,128)S(1)} %mul.214), kind=kLoop, calls=%fused_computation.66 | loop fusion | flops 22806528 | bytes 23605248 | tf_op jit(solution)/shard_map/convert_element_type | solution.py:90
  26.0 15.7 %collective-permute-start.2 = (bf16[3,8,64,256]{3,2,1,0:T(8,128)(2,1)S(1)}, bf16[3,8,64,256]{3,2,1,0:T(8,128)(2,1)S(1)}, u32[]{:S(2)}, u32[]{:S(2)}) collective-permute-start(bf16[3,8,64,256]{3,2,1,0:T(8,128)(2,1)S(1)} %get-tuple-element.11), channel_id=1, source_target_pairs={{0,1},{1,2},{2,3},{3,4},{4,5},{5,6},{6,7},{7,8},{8,9},{9,10},{10,1... | collective-permute-start | bytes 2359304 | tf_op jit(solution)/shard_map/ppermute | solution.py:30
  41.7 1.3 collective-permute-start.3
  43.0 0.5 collective-permute-done.2
  43.5 4.2 collective-permute-done.3
  47.7 0.7 convert_multiply_fusion.2
  48.5 2.0 slice.365
  50.5 18.8 %fusion.95 = bf16[6,8,64,256]{3,2,1,0:T(8,128)(2,1)S(1)} fusion(bf16[6,8,64,256]{3,2,1,0:T(8,128)(2,1)S(1)} %copy-done, f32[6,8,64,256]{3,2,1,0:T(8,128)} %slice.365, f32[12,8,64,256]{3,2,1,0:T(8,128)S(1)} %convert_multiply_fusion.2, f32[6,8,64]{2,1,0:T(8,128)S(1)} %mul.214), kind=kLoop, calls=%fused_computation.162 | loop fusion | flops 24379392 | bytes 25178112 | tf_op jit(solution)/shard_map/convert_element_type | solution.py:96
  69.5 15.6 %collective-permute-start.4 = (bf16[3,8,64,256]{3,2,1,0:T(8,128)(2,1)S(1)}, bf16[3,8,64,256]{3,2,1,0:T(8,128)(2,1)S(1)}, u32[]{:S(2)}, u32[]{:S(2)}) collective-permute-start(bf16[3,8,64,256]{3,2,1,0:T(8,128)(2,1)S(1)} %get-tuple-element.9), channel_id=1, source_target_pairs={{0,1},{1,2},{2,3},{3,4},{4,5},{5,6},{6,7},{7,8},{8,9},{9,10},{10,1... | collective-permute-start | bytes 2359304 | tf_op jit(solution)/shard_map/ppermute | solution.py:30
  85.1 1.3 collective-permute-start.5
  86.4 0.5 collective-permute-done.4
  87.0 4.3 collective-permute-done.5
  91.2 0.7 convert_multiply_fusion.1
  92.0 2.0 slice.374
  94.0 18.8 %fusion.94 = bf16[6,8,64,256]{3,2,1,0:T(8,128)(2,1)S(1)} fusion(bf16[6,8,64,256]{3,2,1,0:T(8,128)(2,1)S(1)} %fusion.11, f32[6,8,64,256]{3,2,1,0:T(8,128)} %slice.374, f32[12,8,64,256]{3,2,1,0:T(8,128)S(1)} %convert_multiply_fusion.1, f32[6,8,64]{2,1,0:T(8,128)S(1)} %mul.214), kind=kLoop, calls=%fused_computation.161 | loop fusion | flops 24379392 | bytes 25178112 | tf_op jit(solution)/shard_map/convert_element_type | solution.py:96
  113.0 15.6 %collective-permute-start.6 = (bf16[3,8,64,256]{3,2,1,0:T(8,128)(2,1)S(1)}, bf16[3,8,64,256]{3,2,1,0:T(8,128)(2,1)S(1)}, u32[]{:S(2)}, u32[]{:S(2)}) collective-permute-start(bf16[3,8,64,256]{3,2,1,0:T(8,128)(2,1)S(1)} %get-tuple-element.6), channel_id=1, source_target_pairs={{0,1},{1,2},{2,3},{3,4},{4,5},{5,6},{6,7},{7,8},{8,9},{9,10},{10,1... | collective-permute-start | bytes 2359304 | tf_op jit(solution)/shard_map/ppermute | solution.py:30
  128.7 1.3 collective-permute-start.7
  130.0 0.6 compare_convert_fusion.1
  130.5 4.2 collective-permute-done.7
  134.8 0.7 convert_multiply_fusion
  135.9 6.8 %fusion.93 = bf16[6,8,64,256]{3,2,1,0:T(8,128)(2,1)S(1)} fusion(bf16[6,8,64,256]{3,2,1,0:T(8,128)(2,1)S(1)} %fusion.95, f32[6,8,64,256]{3,2,1,0:T(8,128)S(1)} %slice.383, f32[12,8,64,256]{3,2,1,0:T(8,128)S(1)} %convert_multiply_fusion, f32[6,8,64]{2,1,0:T(8,128)S(1)} %mul.214), kind=kLoop, calls=%fused_computation.160 | loop fusion | flops 24379392 | bytes 25178112 | tf_op jit(solution)/shard_map/convert_element_type | solution.py:96
  143.0 0.9 broadcast_multiply_fusion.2
  144.2 1.2 fusion.110
  146.0 85.1 %all-gather.4.cloned.1.call-done = f32[16,8,128,128]{3,2,1,0:T(8,128)} async-done(((f32[1,8,128,128]{3,2,1,0:T(8,128)}), f32[16,8,128,128]{3,2,1,0:T(8,128)}) %all-gather.4.cloned.1.call-update) | async-done | bytes 8388624 | tf_op jit(solution)/shard_map/all_gather | solution.py:18
  231.1 3.9 reduce_sum.63
  235.4 11.7 %cholesky.44 = f32[128,128]{1,0:T(8,128)S(1)} custom-call(f32[128,128]{1,0:T(8,128)S(1)} %fusion.108), custom_call_target="Cholesky" | custom-call | tf_op jit(solution)/shard_map/jit(cholesky)/cholesky | solution.py:128
  247.2 0.6 compare_reduce_fusion.1
  247.8 0.7 fusion.103
  248.5 9.8 %custom-call.6 = f32[1,128,128]{1,2,0:T(8,128)S(1)} custom-call(f32[1,128,128]{2,1,0:T(8,128)S(1)} %fusion.103), custom_call_target="InvertDiagBlocksLowerTriangular" | custom-call | tf_op jit(solution)/shard_map/jit(_solve_triangular)/triangular_solve | solution.py:129
  259.3 0.9 broadcast_multiply_fusion.1
  260.5 72.8 %all-gather.6.cloned.1.call-done = f32[16,8,128,128]{3,2,1,0:T(8,128)} async-done(((f32[1,8,128,128]{3,2,1,0:T(8,128)}), f32[16,8,128,128]{3,2,1,0:T(8,128)}) %all-gather.6.cloned.1.call-update) | async-done | bytes 8388624 | tf_op jit(solution)/shard_map/all_gather | solution.py:18
  333.3 3.9 reduce_sum.66
  337.4 0.4 fusion
  337.8 0.4 fusion.116
  338.3 0.9 broadcast_multiply_fusion
  339.2 73.0 %all-gather.8.cloned.1.call-done = f32[16,8,128,128]{3,2,1,0:T(8,128)} async-done(((f32[1,8,128,128]{3,2,1,0:T(8,128)}), f32[16,8,128,128]{3,2,1,0:T(8,128)}) %all-gather.8.cloned.1.call-update) | async-done | bytes 8388624 | tf_op jit(solution)/shard_map/all_gather | solution.py:18
  412.2 3.9 reduce_sum.68
  416.5 11.7 %cholesky.55 = f32[128,128]{1,0:T(8,128)S(1)} custom-call(f32[128,128]{1,0:T(8,128)S(1)} %fusion.106), custom_call_target="Cholesky" | custom-call | tf_op jit(solution)/shard_map/jit(cholesky)/cholesky | solution.py:128
  428.2 0.6 compare_reduce_fusion
  428.9 0.7 fusion.104
  429.5 9.8 %custom-call.7 = f32[1,128,128]{1,2,0:T(8,128)S(1)} custom-call(f32[1,128,128]{2,1,0:T(8,128)S(1)} %fusion.104), custom_call_target="InvertDiagBlocksLowerTriangular" | custom-call | tf_op jit(solution)/shard_map/jit(_solve_triangular)/triangular_solve | solution.py:129
  440.1 1.6 copy.18
  (45 shorter events, 4.8 us)
Async XLA Ops:
  6.5 11.7 %copy-start = (bf16[6,8,64,256]{3,2,1,0:T(8,128)(2,1)S(1)}, bf16[6,8,64,256]{3,2,1,0:T(8,128)(2,1)}, u32[]{:S(2)}) copy-start(bf16[6,8,64,256]{3,2,1,0:T(8,128)(2,1)} %param.6) | copy-start | bytes 4718596
  6.5 6.6 %copy-start.2 = (s32[16]{0:T(128)S(1)}, s32[16]{0:T(128)}, u32[]{:S(2)}) copy-start(s32[16]{0:T(128)} %param.8) | copy-start | bytes 196
  6.5 9.6 %copy-start.1 = (f32[6,512]{1,0:T(8,128)S(1)}, f32[6,512]{1,0:T(8,128)}, u32[]{:S(2)}) copy-start(f32[6,512]{1,0:T(8,128)} %param.7) | copy-start | bytes 36868
  6.5 224.6 %all-gather.4.cloned.1.call-start = ((), (), s32[]{:S(2)}) async-start(), calls=%async_computation | async-start | bytes 8912896 | tf_op jit(solution)/shard_map/all_gather | solution.py:18
  9.3 6.9 %collective-permute-start = (bf16[3,8,64,256]{3,2,1,0:T(8,128)(2,1)}, bf16[3,8,64,256]{3,2,1,0:T(8,128)(2,1)S(1)}, u32[]{:S(2)}, u32[]{:S(2)}) collective-permute-start(bf16[3,8,64,256]{3,2,1,0:T(8,128)(2,1)} %get-tuple-element.13), channel_id=1, source_target_pairs={{0,1},{1,2},{2,3},{3,4},{4,5},{5,6},{6,7},{7,8},{8,9},{9,10},{10,1... | collective-permute-start | bytes 2359304 | tf_op jit(solution)/shard_map/ppermute | solution.py:30
  11.8 6.5 %collective-permute-start.1 = (bf16[3,8,64,256]{3,2,1,0:T(8,128)(2,1)}, bf16[3,8,64,256]{3,2,1,0:T(8,128)(2,1)S(1)}, u32[]{:S(2)}, u32[]{:S(2)}) collective-permute-start(bf16[3,8,64,256]{3,2,1,0:T(8,128)(2,1)} %get-tuple-element.14), channel_id=1, source_target_pairs={{1,0},{2,1},{3,2},{4,3},{5,4},{6,5},{7,6},{8,7},{9,8},{10,9},{11,1... | collective-permute-start | bytes 2359304 | tf_op jit(solution)/shard_map/ppermute | solution.py:33
  26.0 17.6 %collective-permute-start.2 = (bf16[3,8,64,256]{3,2,1,0:T(8,128)(2,1)S(1)}, bf16[3,8,64,256]{3,2,1,0:T(8,128)(2,1)S(1)}, u32[]{:S(2)}, u32[]{:S(2)}) collective-permute-start(bf16[3,8,64,256]{3,2,1,0:T(8,128)(2,1)S(1)} %get-tuple-element.11), channel_id=1, source_target_pairs={{0,1},{1,2},{2,3},{3,4},{4,5},{5,6},{6,7},{7,8},{8,9},{9,10},{10,1... | collective-permute-start | bytes 2359304 | tf_op jit(solution)/shard_map/ppermute | solution.py:30
  41.7 6.0 %collective-permute-start.3 = (bf16[3,8,64,256]{3,2,1,0:T(8,128)(2,1)S(1)}, bf16[3,8,64,256]{3,2,1,0:T(8,128)(2,1)S(1)}, u32[]{:S(2)}, u32[]{:S(2)}) collective-permute-start(bf16[3,8,64,256]{3,2,1,0:T(8,128)(2,1)S(1)} %get-tuple-element.12), channel_id=1, source_target_pairs={{1,0},{2,1},{3,2},{4,3},{5,4},{6,5},{7,6},{8,7},{9,8},{10,9},{11,1... | collective-permute-start | bytes 2359304 | tf_op jit(solution)/shard_map/ppermute | solution.py:33
  69.5 17.5 %collective-permute-start.4 = (bf16[3,8,64,256]{3,2,1,0:T(8,128)(2,1)S(1)}, bf16[3,8,64,256]{3,2,1,0:T(8,128)(2,1)S(1)}, u32[]{:S(2)}, u32[]{:S(2)}) collective-permute-start(bf16[3,8,64,256]{3,2,1,0:T(8,128)(2,1)S(1)} %get-tuple-element.9), channel_id=1, source_target_pairs={{0,1},{1,2},{2,3},{3,4},{4,5},{5,6},{6,7},{7,8},{8,9},{9,10},{10,1... | collective-permute-start | bytes 2359304 | tf_op jit(solution)/shard_map/ppermute | solution.py:30
  85.1 6.1 %collective-permute-start.5 = (bf16[3,8,64,256]{3,2,1,0:T(8,128)(2,1)S(1)}, bf16[3,8,64,256]{3,2,1,0:T(8,128)(2,1)S(1)}, u32[]{:S(2)}, u32[]{:S(2)}) collective-permute-start(bf16[3,8,64,256]{3,2,1,0:T(8,128)(2,1)S(1)} %get-tuple-element.10), channel_id=1, source_target_pairs={{1,0},{2,1},{3,2},{4,3},{5,4},{6,5},{7,6},{8,7},{9,8},{10,9},{11,1... | collective-permute-start | bytes 2359304 | tf_op jit(solution)/shard_map/ppermute | solution.py:33
  113.0 17.5 %collective-permute-start.6 = (bf16[3,8,64,256]{3,2,1,0:T(8,128)(2,1)S(1)}, bf16[3,8,64,256]{3,2,1,0:T(8,128)(2,1)S(1)}, u32[]{:S(2)}, u32[]{:S(2)}) collective-permute-start(bf16[3,8,64,256]{3,2,1,0:T(8,128)(2,1)S(1)} %get-tuple-element.6), channel_id=1, source_target_pairs={{0,1},{1,2},{2,3},{3,4},{4,5},{5,6},{6,7},{7,8},{8,9},{9,10},{10,1... | collective-permute-start | bytes 2359304 | tf_op jit(solution)/shard_map/ppermute | solution.py:30
  128.7 6.1 %collective-permute-start.7 = (bf16[3,8,64,256]{3,2,1,0:T(8,128)(2,1)S(1)}, bf16[3,8,64,256]{3,2,1,0:T(8,128)(2,1)S(1)}, u32[]{:S(2)}, u32[]{:S(2)}) collective-permute-start(bf16[3,8,64,256]{3,2,1,0:T(8,128)(2,1)S(1)} %get-tuple-element.8), channel_id=1, source_target_pairs={{1,0},{2,1},{3,2},{4,3},{5,4},{6,5},{7,6},{8,7},{9,8},{10,9},{11,1... | collective-permute-start | bytes 2359304 | tf_op jit(solution)/shard_map/ppermute | solution.py:33
  144.0 189.3 %all-gather.6.cloned.1.call-start = ((), (), s32[]{:S(2)}) async-start(), calls=%async_computation.1 | async-start | bytes 8912896 | tf_op jit(solution)/shard_map/all_gather | solution.py:18
  260.2 152.0 %all-gather.8.cloned.1.call-start = ((), (), s32[]{:S(2)}) async-start(), calls=%async_computation.2 | async-start | bytes 8912896 | tf_op jit(solution)/shard_map/all_gather | solution.py:18
Sparse Core Ops, SparseCore 0:
  144.1 87.0 all-gather.3
  260.4 72.8 all-gather.5
  339.3 72.8 all-gather.7
